TPU v7x, 512 devices: a whole 4x8x8 slice. The times are simulated.
512 devices in a mesh: rows: 32 (over y, x), vocab: 16 (over z, core).
Axes of the slice: x: 4, y: 8, z: 8, core: 2. Of those that a mesh axis runs over, the one named last changes fastest.
Arguments:
- hidden: bfloat16 [12288, 8192], P('rows', 'vocab'), may hold values from -128 to 128
- head: bfloat16 [8192, 8192], P('rows', 'vocab'), may hold values from -4 to 4
- targets: int32 [12288], P('rows'), may hold values from 0 to 128255
- live: int32 [12288], P('rows'), may hold values from 0 to 1, as said below
- prior_lse: float32 [12288], P('rows'), may hold values from 10 to 18
- prior_mean: float32 [12288], P('rows'), may hold values from 2 to 8
- prior_target: float32 [12288], P('rows'), may hold values from -12 to 12
- seq_lengths: int32 [32], replicated, may hold values from 1 to 768, 12288 in all
Outputs:
- logprob: float32 [12288], P(('rows', 'vocab'))
- entropy: float32 [12288], P(('rows', 'vocab'))
- seq_score: float32 [32], replicated
Inputs may be any that keep to these rules, and one draw needn't show every extreme that they name: Within the 384 rows of each index of rows, the live rows come first; every such index has at least 48 live rows and some index has all 384.
All inputs are finite; a program needn't handle non-finite values.
Results may differ from a plain program's by a relative error of at most 0.0003.
Values may be sent and summed in bfloat16 or wider, within the bound.
No kernel may reach another device: no remote copies, remote signals or barrier semaphores. Data moves between devices by JAX's collectives and lax.ppermute only.
A program may use at most 64 MiB of HBM per device.

v0:
```python
import jax
import jax.numpy as jnp
from jax import lax
from jax.sharding import PartitionSpec as P

VOCAB = 128256
SEQS = 32
GSIZE = 8


def finish_rows(block_peak, block_mass, block_moment, block_target, live, prior_lse, prior_mean):
    highest = jnp.maximum(block_peak, prior_lse)
    earlier = jnp.exp(prior_lse - highest)
    scaled = jnp.exp(block_peak - highest)
    total_mass = earlier + block_mass * scaled
    norm_log = highest + jnp.log(total_mass)
    average = (earlier * prior_mean + scaled * block_moment) / total_mass
    keeping = live.astype(jnp.float32)
    return (keeping * (block_target - norm_log), keeping * (norm_log - average))


def local(hidden, head, targets, live, prior_lse, prior_mean, prior_target, seq_lengths):
    rows_here = hidden.shape[0]
    cols_here = head.shape[1]
    spread = lax.axis_size("vocab")
    which = lax.axis_index("vocab")
    block_first = VOCAB - cols_here * spread
    first_col = block_first + which * cols_here
    gathered = lax.all_gather(hidden, "vocab", axis=1, tiled=True)
    logits = jnp.dot(
        gathered,
        lax.all_gather(head, "rows", axis=0, tiled=True),
        preferred_element_type=jnp.float32,
    )
    row_peak = jnp.max(logits, axis=1)
    weights = jnp.exp(logits - row_peak[:, None])
    row_mass = jnp.sum(weights, axis=1)
    moment = jnp.sum(weights * logits, axis=1)
    column = targets - first_col
    columns = lax.broadcasted_iota(jnp.int32, logits.shape, 1)
    picked = jnp.sum(jnp.where(columns == column[:, None], logits, jnp.zeros_like(logits)), axis=1)
    share = rows_here // spread
    begin = which * share

    def own_rows(values):
        return lax.dynamic_slice_in_dim(values, begin, share, 0)

    highest = lax.pmax(row_peak, "vocab")
    factor = jnp.exp(row_peak - highest)
    mass_all, moment_all, picked_all = lax.psum(
        (row_mass * factor, moment * factor, picked), "vocab"
    )
    peak_share = own_rows(highest)
    mass_share = own_rows(mass_all)
    moment_share = own_rows(moment_all)
    picked_share = own_rows(picked_all)
    target_share = own_rows(targets)
    block_target = jnp.where(target_share >= block_first, picked_share, own_rows(prior_target))
    logprob, entropy = finish_rows(
        peak_share,
        mass_share,
        moment_share,
        block_target,
        own_rows(live),
        own_rows(prior_lse),
        own_rows(prior_mean),
    )
    global_rows = lax.axis_index("rows") * rows_here + begin + jnp.arange(share, dtype=jnp.int32)
    endings = jnp.cumsum(seq_lengths)
    member = jnp.sum((global_rows[:, None] >= endings[None, :]).astype(jnp.int32), axis=1)
    onehot = (member[:, None] == jnp.arange(SEQS, dtype=jnp.int32)[None, :]).astype(jnp.float32)
    partial_sums = jnp.sum(onehot * logprob[:, None], axis=0)
    sums = lax.psum(partial_sums, ("rows", "vocab"))
    seq_mean = sums / seq_lengths.astype(jnp.float32)
    grouped = seq_mean.reshape(SEQS // GSIZE, GSIZE)
    seq_score = (grouped - jnp.mean(grouped, axis=1, keepdims=True)).reshape(SEQS)
    return (logprob, entropy, seq_score)


def solution(mesh):
    return jax.shard_map(
        local,
        mesh=mesh,
        in_specs=(
            P("rows", "vocab"),
            P("rows", "vocab"),
            P("rows"),
            P("rows"),
            P("rows"),
            P("rows"),
            P("rows"),
            P(),
        ),
        out_specs=(P(("rows", "vocab")), P(("rows", "vocab")), P()),
        check_vma=False,
    )
```

profile of v0, /device:TPU:1, one launch (start us, length us, event | category | flops | bytes accessed | tf_op | source)
XLA Modules:
  0.0 332.5 jit_solution(5648980550424565232)
XLA Ops:
  7.2 0.0 all-gather.3.cloned.1.call-start
  7.2 0.7 all-gather.3.cloned.1.call-update
  7.9 0.0 all-gather.5.cloned.1.call-start
  7.9 0.7 all-gather.5.cloned.1.call-update
  8.7 0.7 copy.13
  9.4 0.1 reduce-window.8
  9.4 0.1 reduce
  9.6 0.2 convert_reduce_fusion
  9.8 0.7 broadcast_subtract_fusion
  10.4 0.0 copy-start
  10.4 55.1 %all-gather.3.cloned.1.call-done = bf16[384,8192]{1,0:T(8,128)(2,1)} async-done(((bf16[384,512]{1,0:T(8,128)(2,1)}), bf16[384,8192]{1,0:T(8,128)(2,1)}) %all-gather.3.cloned.1.call-update) | async-done | bytes 6291472 | tf_op jit(solution)/shard_map/all_gather | solution.py:29
  65.6 103.9 %all-gather.5.cloned.1.call-done = bf16[8192,512]{1,0:T(8,128)(2,1)} async-done(((bf16[256,512]{1,0:T(8,128)(2,1)}), bf16[8192,512]{1,0:T(8,128)(2,1)}) %all-gather.5.cloned.1.call-update) | async-done | bytes 8388624 | tf_op jit(solution)/shard_map/all_gather | solution.py:32
  169.4 8.0 %fusion.5 = (f32[384]{0:T(512)S(1)}, f32[384,512]{1,0:T(8,128)S(1)}) fusion(bf16[384,8192]{1,0:T(8,128)(2,1)} %all-gather.3.cloned.1.call-done, bf16[8192,512]{1,0:T(8,128)(2,1)} %all-gather.5.cloned.1.call-done), kind=kOutput, calls=%fused_computation.24 | convolution fusion | flops 3221421568 | bytes 15468032 | tf_op jit(solution)/shard_map/dot_general | solution.py:30
  177.4 25.1 %pmax.7 = f32[384]{0:T(512)S(1)} all-reduce(f32[384]{0:T(512)S(1)} %get-tuple-element.13), channel_id=1, replica_groups=mesh['rows'=32,'vocab'=16] {'vocab'}, use_global_device_ids=true, to_apply=%region_3.4 | all-reduce | flops 384 | bytes 3072 | tf_op jit(solution)/shard_map/pmax | solution.py:48
  202.5 0.5 multiply_reduce_fusion
  203.0 25.8 %all-reduce = (f32[384]{0:T(512)S(1)}, f32[384]{0:T(512)S(1)}, f32[384]{0:T(512)S(1)}) all-reduce(f32[384]{0:T(512)S(1)} %get-tuple-element.5, f32[384]{0:T(512)S(1)} %get-tuple-element.12, f32[384]{0:T(512)S(1)} %get-tuple-element.11), channel_id=1, replica_groups=mesh['rows'=32,'vocab'=16] {'vocab'}, use_global_device_ids=true, to_apply=%region_1.0 | all-reduce | flops 1152 | bytes 9216 | tf_op jit(solution)/shard_map/psum | solution.py:50
  228.9 1.4 subtract_multiply_fusion
  230.2 0.0 copy-start.1
  230.2 0.1 select_reduce_fusion.1
  230.3 94.4 %psum.31 = f32[32]{0:T(128)S(1)} all-reduce(f32[32]{0:T(128)S(1)} %select_reduce_fusion.1), channel_id=1, replica_groups=mesh['rows'=32,'vocab'=16] {'rows','vocab'}, use_global_device_ids=true, to_apply=%region_11.12 | all-reduce | flops 32 | bytes 256 | tf_op jit(solution)/shard_map/psum | solution.py:73
  324.7 0.0 copy-done
  324.7 0.1 reshape.49
  324.8 0.1 reduce_sum.59
  325.0 0.1 sub.49
  325.0 0.1 sub.50
  325.1 0.5 sub.51
  325.6 0.0 copy-done.1
  (4 shorter events, 0.0 us)
Async XLA Ops:
  7.2 58.4 %all-gather.3.cloned.1.call-start = ((), (), s32[]{:S(2)}) async-start(), calls=%async_computation | async-start | bytes 6684672 | tf_op jit(solution)/shard_map/all_gather | solution.py:29
  7.9 161.5 %all-gather.5.cloned.1.call-start = ((), (), s32[]{:S(2)}) async-start(), calls=%async_computation.1 | async-start | bytes 8650752 | tf_op jit(solution)/shard_map/all_gather | solution.py:32
  10.4 314.3 %copy-start = (s32[32]{0:T(128)S(1)}, s32[32]{0:T(128)}, u32[]{:S(2)}) copy-start(s32[32]{0:T(128)} %param.15) | copy-start | bytes 388
  230.2 95.4 %copy-start.1 = (f32[24]{0:T(128)}, f32[24]{0:T(128)S(1)}, u32[]{:S(2)}) copy-start(f32[24]{0:T(128)S(1)} %get-tuple-element.10) | copy-start | bytes 292
Sparse Core Ops, SparseCore 0:
  10.1 55.3 all-gather.2
  68.7 100.6 all-gather.4
where the time goes:
time: 333 us; the launch traced here: 332 us
  waiting for transfers between devices  160 us (48%)
  blocking collectives  145 us (44%)
  between operations  14.1 us (4%)
  matrix products  8 us (2%)
  other arithmetic  3.64 us (1%)
    all_gather x1, waiting for transfers between devices, local(): lax.all_gather(head, 'rows', axis=0, tiled=True)  104 us
    psum x1, blocking collectives, local(): sums = lax.psum(partial_sums, ('rows', 'vocab'))  94.4 us
    all_gather x1, waiting for transfers between devices, local(): gathered = lax.all_gather(hidden, 'vocab', axis=1, tiled=True)  55.1 us
    psum x1, blocking collectives, local(): lax.psum((row_mass * factor, moment * factor, picked), 'vocab')  25.8 us
    pmax x1, blocking collectives, local(): highest = lax.pmax(row_peak, 'vocab')  25.1 us
    dot_general x1, matrix products, local(): jnp.dot(gathered, lax.all_gather(head, 'rows', axis=0, tiled=True), prefe...  8 us
  transfers between devices with their start and end apart: 2, of which 2 were waited for; matrix products, arithmetic and copies ran while one was open for 1% of the time, Pallas kernels for 0%

commit v1 on v0

--- a/solution.py
+++ b/solution.py
@@ -70,7 +70,12 @@
     member = jnp.sum((global_rows[:, None] >= endings[None, :]).astype(jnp.int32), axis=1)
     onehot = (member[:, None] == jnp.arange(SEQS, dtype=jnp.int32)[None, :]).astype(jnp.float32)
     partial_sums = jnp.sum(onehot * logprob[:, None], axis=0)
-    sums = lax.psum(partial_sums, ("rows", "vocab"))
+
+    def object_watch(raw):
+        vec_out = lax.all_gather(raw, axis_name=("rows", "vocab")).sum(axis=0)
+        return vec_out
+
+    sums = object_watch(partial_sums)
     seq_mean = sums / seq_lengths.astype(jnp.float32)
     grouped = seq_mean.reshape(SEQS // GSIZE, GSIZE)
     seq_score = (grouped - jnp.mean(grouped, axis=1, keepdims=True)).reshape(SEQS)

time: 333 us -> 494 us (1.48)
  waiting for transfers between devices: 160 us -> 415 us
  blocking collectives: 145 us -> 50.9 us
    unnamed x2 -> x4, waiting for transfers between devices: 1.38 us -> 256 us
    psum x1 -> x0, blocking collectives: 94.4 us -> none  [local(): sums = lax.psum(partial_sums, ('rows', 'vocab'))]
  transfers between devices with their start and end apart: 2 -> 3, of which waited for: 2 -> 3; matrix products, arithmetic and copies ran while one was open for 1% -> 0% of each run, Pallas kernels for 0% -> 0%
where the time goes in v1:
time: 494 us
  waiting for transfers between devices  415 us (84%)
  blocking collectives  50.9 us (10%)
  between operations  13.8 us (3%)
  matrix products  8 us (2%)
    unnamed x4, waiting for transfers between devices  256 us
    all_gather x1, waiting for transfers between devices, local(): lax.all_gather(head, 'rows', axis=0, tiled=True)  104 us
    all_gather x1, waiting for transfers between devices, local(): gathered = lax.all_gather(hidden, 'vocab', axis=1, tiled=True)  55 us
    psum x1, blocking collectives, local(): lax.psum((row_mass * factor, moment * factor, picked), 'vocab')  25.8 us
    pmax x1, blocking collectives, local(): highest = lax.pmax(row_peak, 'vocab')  25.1 us
  transfers between devices with their start and end apart: 3, of which 3 were waited for; matrix products, arithmetic and copies ran while one was open for 0% of the time, Pallas kernels for 0%

profile of v1, /device:TPU:1, one launch (start us, length us, event | category | flops | bytes accessed | tf_op | source)
XLA Modules:
  0.0 494.0 jit_solution(16859396387170751881)
XLA Ops:
  7.2 0.0 all-gather.4.cloned.1.call-start
  7.2 0.7 all-gather.4.cloned.1.call-update
  7.9 0.0 all-gather.6.cloned.1.call-start
  7.9 0.7 all-gather.6.cloned.1.call-update
  8.6 0.0 all-reduce.4.cloned.1.call-start
  8.7 0.7 copy.13
  9.4 0.1 reduce-window.8
  9.5 0.1 reduce
  9.6 0.2 convert_reduce_fusion
  9.8 0.7 broadcast_subtract_fusion
  10.5 0.0 copy-start.1
  10.5 55.0 %all-gather.4.cloned.1.call-done = bf16[384,8192]{1,0:T(8,128)(2,1)} async-done(((bf16[384,512]{1,0:T(8,128)(2,1)}), bf16[384,8192]{1,0:T(8,128)(2,1)}) %all-gather.4.cloned.1.call-update) | async-done | bytes 6291472 | tf_op jit(solution)/shard_map/all_gather | solution.py:29
  65.6 103.9 %all-gather.6.cloned.1.call-done = bf16[8192,512]{1,0:T(8,128)(2,1)} async-done(((bf16[256,512]{1,0:T(8,128)(2,1)}), bf16[8192,512]{1,0:T(8,128)(2,1)}) %all-gather.6.cloned.1.call-update) | async-done | bytes 8388624 | tf_op jit(solution)/shard_map/all_gather | solution.py:32
  169.4 8.0 %fusion.5 = (f32[384]{0:T(512)S(1)}, f32[384,512]{1,0:T(8,128)S(1)}) fusion(bf16[384,8192]{1,0:T(8,128)(2,1)} %all-gather.4.cloned.1.call-done, bf16[8192,512]{1,0:T(8,128)(2,1)} %all-gather.6.cloned.1.call-done), kind=kOutput, calls=%fused_computation.24 | convolution fusion | flops 3221421568 | bytes 15468032 | tf_op jit(solution)/shard_map/dot_general | solution.py:30
  177.4 25.1 %pmax.7 = f32[384]{0:T(512)S(1)} all-reduce(f32[384]{0:T(512)S(1)} %get-tuple-element.13), channel_id=1, replica_groups=mesh['rows'=32,'vocab'=16] {'vocab'}, use_global_device_ids=true, to_apply=%region_3.4 | all-reduce | flops 384 | bytes 3072 | tf_op jit(solution)/shard_map/pmax | solution.py:48
  202.5 0.5 multiply_reduce_fusion
  203.0 25.8 %all-reduce.1 = (f32[384]{0:T(512)S(1)}, f32[384]{0:T(512)S(1)}, f32[384]{0:T(512)S(1)}) all-reduce(f32[384]{0:T(512)S(1)} %get-tuple-element.5, f32[384]{0:T(512)S(1)} %get-tuple-element.12, f32[384]{0:T(512)S(1)} %get-tuple-element.11), channel_id=1, replica_groups=mesh['rows'=32,'vocab'=16] {'vocab'}, use_global_device_ids=true, to_apply=%region_1.0 | all-reduce | flops 1152 | bytes 9216 | tf_op jit(solution)/shard_map/psum | solution.py:50
  228.9 1.4 subtract_multiply_fusion
  230.2 0.1 select_reduce_fusion.1
  230.3 0.3 dynamic-update-slice
  230.6 0.6 copy-done
  231.2 0.0 all-reduce.4.cloned.1.call-update
  231.3 254.3 %all-reduce.4.cloned.1.call-done = f32[16384]{0:T(1024)} async-done(((f32[16384]{0:T(1024)}), f32[16384]{0:T(1024)}) %all-reduce.4.cloned.1.call-update) | async-done | bytes 65552
  485.5 0.9 reshape.50
  486.5 0.1 reduce_sum.68
  486.6 0.0 copy-done.1
  486.6 0.1 reshape.49
  486.7 0.1 reduce_sum.69
  486.8 0.1 sub.49
  486.9 0.1 sub.50
  487.0 0.5 sub.51
  487.5 0.0 copy-done.2
  (7 shorter events, 0.0 us)
Async XLA Ops:
  7.2 58.4 %all-gather.4.cloned.1.call-start = ((), (), s32[]{:S(2)}) async-start(), calls=%async_computation | async-start | bytes 6684672 | tf_op jit(solution)/shard_map/all_gather | solution.py:29
  7.9 161.5 %all-gather.6.cloned.1.call-start = ((), (), s32[]{:S(2)}) async-start(), calls=%async_computation.1 | async-start | bytes 8650752 | tf_op jit(solution)/shard_map/all_gather | solution.py:32
  8.6 476.9 %all-reduce.4.cloned.1.call-start = ((), (), s32[]{:S(2)}) async-start(), calls=%async_computation.2 | async-start | bytes 131072
  10.5 476.1 %copy-start.1 = (s32[32]{0:T(128)S(1)}, s32[32]{0:T(128)}, u32[]{:S(2)}) copy-start(s32[32]{0:T(128)} %param.15) | copy-start | bytes 388
  230.2 257.2 %copy-start.2 = (f32[24]{0:T(128)}, f32[24]{0:T(128)S(1)}, u32[]{:S(2)}) copy-start(f32[24]{0:T(128)S(1)} %get-tuple-element.10) | copy-start | bytes 292
  230.6 0.6 copy-start
Sparse Core Ops, SparseCore 0:
  10.1 55.3 all-gather.3
  68.7 100.6 all-gather.5
  231.4 254.1 all-reduce.3
